TPU v7x, 32 devices: a whole 2x2x4 slice. The times are simulated.
32 devices in a mesh: row: 8 (over z, y), col: 4 (over x, core).
Axes of the slice: x: 2, y: 2, z: 4, core: 2. Of those that a mesh axis runs over, the one named last changes fastest.
Arguments:
- density: float32 [4, 256, 2048], P('col', 'row'), may hold values from 0.5 to 2
- momentum: float32 [3, 4, 256, 2048], P(None, 'col', 'row'), may hold values from -6 to 6
- energy: float32 [4, 256, 2048], P('col', 'row'), may hold values from 2 to 5
Outputs:
- tendency: float32 [5, 4, 256, 2048], P(None, 'col', 'row')
All inputs are finite; a program needn't handle non-finite values.
Results may differ from a plain program's by a relative error of at most 0.000053.
Values sent between devices are 32-bit elements; how exact they have to be, the bound alone decides.
No kernel may reach another device: no remote copies, remote signals or barrier semaphores. Data moves between devices by JAX's collectives and lax.ppermute only.
A program may use at most 64 MiB of HBM per device.

v0:
```python
import jax
import jax.numpy as jnp
import numpy as np
from jax import lax
from jax.sharding import PartitionSpec as P


def operator_column(count):
    steps = np.arange(count)
    wave = 2.0 * np.pi * steps / count
    upper = (
        17.0 / 12.0 * np.sin(wave)
        + 101.0 / 300.0 * np.sin(2.0 * wave)
        + 1.0 / 300.0 * np.sin(3.0 * wave)
    )
    lower = 1.0 + np.cos(wave) + 0.1 * np.cos(2.0 * wave)
    ratio = upper / lower
    phase = 2.0 * np.pi * (steps[:, None] * steps[None, :] % count) / count
    return -np.sum(ratio[:, None] * np.sin(phase), axis=0) / count


def operator_table(count):
    column = operator_column(count)
    steps = np.arange(count)
    offsets = (steps[None, :] - steps[:, None]) % count
    return column[offsets].astype(np.float32)


def block_weights(count):
    table = operator_table(count)
    width = 128
    w_self = table[:width, :width]
    w_prev = table[:width, width : 2 * width]
    w_next = table[width : 2 * width, :width]
    return jnp.asarray(np.concatenate([w_prev, w_self, w_next], axis=1))


def compact_last(field):
    count = field.shape[-1]
    width = 128
    blocks = field.reshape(field.shape[:-1] + (count // width, width))
    parts = jnp.einsum(
        "...bj,jk->...bk", blocks, block_weights(count), precision=lax.Precision.HIGHEST
    )
    result = (
        jnp.roll(parts[..., :width], 1, axis=-2)
        + parts[..., width : 2 * width]
        + jnp.roll(parts[..., 2 * width :], -1, axis=-2)
    )
    return result.reshape(field.shape)


def compact_second(field):
    count = field.shape[-2]
    if count <= 256:
        weights = jnp.asarray(operator_table(count))
        return jnp.einsum("...jc,ji->...ic", field, weights, precision=lax.Precision.HIGHEST)
    width = 128
    blocks = field.reshape(field.shape[:-2] + (count // width, width, field.shape[-1]))
    parts = jnp.einsum(
        "...bjc,jk->...bkc", blocks, block_weights(count), precision=lax.Precision.HIGHEST
    )
    result = (
        jnp.roll(parts[..., :width, :], 1, axis=-3)
        + parts[..., width : 2 * width, :]
        + jnp.roll(parts[..., 2 * width :, :], -1, axis=-3)
    )
    return result.reshape(field.shape)


def fluxes(density, momentum, energy):
    speed = momentum / density[None]
    pressure = 0.4 * (energy - 0.5 * jnp.sum(momentum * momentum, axis=0) / density)
    enthalpy = energy + pressure
    vel_x, vel_y = (speed[0], speed[1])
    flux_x = jnp.stack(
        [
            momentum[0],
            momentum[0] * vel_x + pressure,
            momentum[1] * vel_x,
            momentum[2] * vel_x,
            enthalpy * vel_x,
        ]
    )
    flux_y = jnp.stack(
        [
            momentum[1],
            momentum[0] * vel_y,
            momentum[1] * vel_y + pressure,
            momentum[2] * vel_y,
            enthalpy * vel_y,
        ],
        axis=2,
    )
    return (flux_x, flux_y)


def local(density, momentum, energy):
    flux_x, flux_y = fluxes(density, momentum, energy)
    planes, owned, length = (flux_y.shape[0], flux_y.shape[1], flux_y.shape[3])
    packed = flux_y.reshape(planes, owned, 5 * length)
    derivative_x = compact_last(flux_x)
    y_lines = lax.all_to_all(packed, "row", split_axis=2, concat_axis=1, tiled=True)
    derivative_lines = compact_second(y_lines)
    derived = lax.all_to_all(derivative_lines, "row", split_axis=1, concat_axis=2, tiled=True)
    derivative_y = jnp.transpose(derived.reshape(planes, owned, 5, length), (2, 0, 1, 3))
    return -(derivative_x + derivative_y)


def solution(mesh):
    in_specs = (P("col", "row", None), P(None, "col", "row", None), P("col", "row", None))
    out_specs = P(None, "col", "row", None)
    return jax.shard_map(local, mesh=mesh, in_specs=in_specs, out_specs=out_specs, check_vma=False)
```

profile of v0, /device:TPU:0, one launch (start us, length us, event | category | flops | bytes accessed | tf_op | source)
XLA Modules:
  0.0 174.0 jit_solution(4821467168655819884)
XLA Ops:
  0.0 0.0 copy-start
  0.0 1.0 bitcast_dynamic-update-slice_fusion.9
  1.0 0.0 copy-start.1
  1.1 0.0 copy-start.2
  1.1 1.4 multiply_reduce_fusion
  2.5 0.0 copy-done
  2.5 0.0 copy-done.1
  2.5 0.0 copy-done.2
  2.5 0.1 bitcast_dynamic-update-slice_fusion.7
  2.7 3.8 %copy.31 = f32[1,32,5,2048]{1,3,2,0:T(8,128)} copy(f32[1,32,5,2048]{3,1,2,0:T(8,128)S(1)} %bitcast_dynamic-update-slice_fusion.5) | data formatting | bytes 2621440 | tf_op jit(solution)/shard_map/reshape | solution.py:101
  6.5 0.5 broadcast.11
  7.0 47.4 %reduce.1 = f32[10240,32]{1,0:T(8,128)} reduce(f32[10240,1,32]{2,1,0:T(1,128)} %bitcast.106, f32[]{:T(128)} %broadcast.11), dimensions={1}, to_apply=%bitcast.93.reduce_sub_computation | reduce | bytes 2621444
  54.4 5.3 %reshape.146 = f32[8,1,40960]{2,1,0:T(1,128)} reshape(f32[10240,32]{1,0:T(8,128)} %reduce.1) | data formatting | bytes 2621440
  59.8 38.7 %all_to_all.30 = f32[8,1,40960]{2,1,0:T(1,128)S(1)} all-to-all(f32[8,1,40960]{2,1,0:T(1,128)} %reshape.146), channel_id=1, replica_groups=mesh['row'=8,'col'=4] {'row'}, dimensions={0} | all-to-all | bytes 2621440 | tf_op jit(solution)/shard_map/all_to_all | solution.py:103
  98.4 5.2 %reduce.2 = f32[8,40960]{1,0:T(8,128)} reduce(f32[8,1,40960]{2,1,0:T(1,128)S(1)} %all_to_all.30, f32[]{:T(128)} %broadcast.11), dimensions={1}, to_apply=%all_to_all.22.reduce_sub_computation | reduce | bytes 2621444 | tf_op jit(solution)/shard_map/all_to_all | solution.py:103
  103.7 12.0 %reshape.147 = f32[10240,1,32]{2,1,0:T(1,128)} reshape(f32[8,40960]{1,0:T(8,128)} %reduce.2) | data formatting | bytes 2621440
  115.6 10.6 %copy.26 = f32[1,32,10240]{2,1,0:T(8,128)} copy(f32[1,32,10240]{1,0,2:T(1,128)} %bitcast.107) | data formatting | bytes 2621440 | tf_op jit(solution)/shard_map/all_to_all | solution.py:103
  126.2 1.5 reshape.141
  127.8 2.2 %convolution_bitcast_fusion = f32[1,256,1280]{2,1,0:T(8,128)S(1)} fusion(f32[256,256]{1,0:T(8,128)} %constant.17, f32[256,1280]{1,0:T(8,128)S(1)} %reshape.141), kind=kOutput, calls=%fused_computation | convolution fusion | flops 1006632960 | bytes 2883584 | tf_op jit(solution)/shard_map/...jc,ji->...ic/dot_general | solution.py:57
  130.0 2.4 %copy.27 = f32[1,256,1280]{2,0,1:T(1,128)} copy(f32[1,256,1280]{2,1,0:T(8,128)S(1)} %convolution_bitcast_fusion) | data formatting | bytes 2621440 | tf_op jit(solution)/shard_map/...jc,ji->...ic/transpose | solution.py:57
  132.4 4.3 %all-to-all-start.1 = ((f32[1,256,1280]{2,0,1:T(1,128)}), f32[1,256,1280]{2,0,1:T(1,128)}, u32[]{:S(2)}, u32[]{:S(2)}) async-start(f32[1,256,1280]{2,0,1:T(1,128)} %copy.27), calls=%async_computation.1 | async-start | bytes 2621440 | tf_op jit(solution)/shard_map/all_to_all | solution.py:105
  136.6 0.1 multiply_bitcast_fusion
  136.9 0.1 fusion.7
  137.1 0.0 copy-start.3
  137.2 0.8 copy-done.3
  138.0 3.5 %convolution_bitcast_fusion.1 = f32[5,1,32,16,384]{4,3,2,0,1:T(8,128)S(1)} fusion(f32[5,32,16,128]{3,2,1,0:T(8,128)S(1)} %bitcast_dynamic-update-slice_fusion, f32[128,384,1,1]{1,0,3,2:T(8,128)S(1)} %copy-done.3), kind=kOutput, calls=%fused_computation.1 | convolution fusion | flops 1509949440 | bytes 5439488 | tf_op jit(solution)/shard_map/...bj,jk->...bk/dot_general | solution.py:42
  141.5 0.1 fusion.10
  141.6 0.2 fusion.9
  141.9 0.4 fusion
  142.2 0.2 reshape.137
  142.4 24.9 %all-to-all-done.1 = f32[1,256,1280]{2,0,1:T(1,128)} async-done(((f32[1,256,1280]{2,0,1:T(1,128)}), f32[1,256,1280]{2,0,1:T(1,128)}, u32[]{:S(2)}, u32[]{:S(2)}) %all-to-all-start.1) | async-done | bytes 1310752 | tf_op jit(solution)/shard_map/all_to_all | solution.py:105
  167.3 3.1 %copy.40 = f32[1,8,32,1280]{3,1,2,0:T(8,128)} copy(f32[1,8,32,1280]{3,0,2,1:T(1,128)} %bitcast.16) | data formatting | bytes 2621440 | tf_op jit(solution)/shard_map/all_to_all | solution.py:105
  170.5 1.5 reshape.140
  172.0 2.0 %fusion.1 = f32[5,1,32,2048]{3,2,1,0:T(8,128)} fusion(f32[5,1,32,2048]{3,2,1,0:T(8,128)S(1)} %reshape.137, f32[1,32,5,2048]{3,2,1,0:T(8,128)S(1)} %reshape.140), kind=kLoop, calls=%fused_computation.5 | loop fusion | flops 655360 | bytes 3932160 | tf_op jit(solution)/shard_map/neg | solution.py:107
  (13 shorter events, 0.4 us)
Async XLA Ops:
  0.0 2.5 %copy-start = (f32[3,1,32,2048]{3,2,1,0:T(8,128)S(1)}, f32[3,1,32,2048]{3,2,1,0:T(8,128)}, u32[]{:S(2)}) copy-start(f32[3,1,32,2048]{3,2,1,0:T(8,128)} %param.6) | copy-start | bytes 2359300
  1.0 1.5 copy-start.1
  1.1 1.5 copy-start.2
  132.4 35.0 %all-to-all-start.1 = ((f32[1,256,1280]{2,0,1:T(1,128)}), f32[1,256,1280]{2,0,1:T(1,128)}, u32[]{:S(2)}, u32[]{:S(2)}) async-start(f32[1,256,1280]{2,0,1:T(1,128)} %copy.27), calls=%async_computation.1 | async-start | bytes 2621440 | tf_op jit(solution)/shard_map/all_to_all | solution.py:105
  137.1 0.9 copy-start.3
where the time goes:
time: 175 us; the launch traced here: 174 us
  other arithmetic  56.7 us (32%)
  local copies, waits for them, and re-layouts  43.5 us (25%)
  blocking collectives  38.7 us (22%)
  waiting for transfers between devices  24.9 us (14%)
  matrix products  5.71 us (3%)
  starting transfers between devices  4.26 us (2%)
    unnamed x6, other arithmetic  47.7 us
    all_to_all x1, blocking collectives, local(): lax.all_to_all(packed, 'row', split_axis=2, concat_axis=1, tiled=True)  38.7 us
    all_to_all x1, waiting for transfers between devices, local(): lax.all_to_all(derivative_lines, 'row', split_axis=1, concat_axis=2, tile...  24.9 us
    unnamed x21, local copies, waits for them, and re-layouts  20 us
    all_to_all x1, local copies, waits for them, and re-layouts, local(): lax.all_to_all(packed, 'row', split_axis=2, concat_axis=1, tiled=True)  10.6 us
    all_to_all x1, other arithmetic, local(): lax.all_to_all(packed, 'row', split_axis=2, concat_axis=1, tiled=True)  5.24 us
    all_to_all x1, starting transfers between devices, local(): lax.all_to_all(derivative_lines, 'row', split_axis=1, concat_axis=2, tile...  4.26 us
    reshape x1, local copies, waits for them, and re-layouts, local(): packed = flux_y.reshape(planes, owned, 5 * length)  3.76 us
  transfers between devices with their start and end apart: 1, of which 1 were waited for; matrix products, arithmetic and copies ran while one was open for 3% of the time, Pallas kernels for 0%

commit v1 on v0

--- a/solution.py
+++ b/solution.py
@@ -3,6 +3,17 @@
 import numpy as np
 from jax import lax
 from jax.sharding import PartitionSpec as P
+
+
+def split_up(array, dim, length):
+    before, after = (array.shape[:dim], array.shape[dim + 1 :])
+    return jnp.moveaxis(array.reshape(*before, length, -1, *after), dim, 0)
+
+
+def laid_out(blocks, dim):
+    blocks = jnp.moveaxis(blocks, 0, dim)
+    dims = blocks.shape
+    return blocks.reshape(*dims[:dim], dims[dim] * dims[dim + 1], *dims[dim + 2 :])
 
 
 def operator_column(count):
@@ -100,7 +111,15 @@
     planes, owned, length = (flux_y.shape[0], flux_y.shape[1], flux_y.shape[3])
     packed = flux_y.reshape(planes, owned, 5 * length)
     derivative_x = compact_last(flux_x)
-    y_lines = lax.all_to_all(packed, "row", split_axis=2, concat_axis=1, tiled=True)
+    size, place = (lax.axis_size("row"), lax.axis_index("row"))
+    blocks_2 = split_up(packed, 2, size)
+    whole = blocks_2
+    for step in range(1, size):
+        target, source = ((place + step) % size, (place - step) % size)
+        sent = lax.dynamic_index_in_dim(blocks_2, target, 0)
+        other = lax.ppermute(sent, "row", [(i, (i + step) % size) for i in range(size)])
+        whole = lax.dynamic_update_slice_in_dim(whole, other, source, axis=0)
+    y_lines = laid_out(whole, 1)
     derivative_lines = compact_second(y_lines)
     derived = lax.all_to_all(derivative_lines, "row", split_axis=1, concat_axis=2, tiled=True)
     derivative_y = jnp.transpose(derived.reshape(planes, owned, 5, length), (2, 0, 1, 3))

time: 175 us -> 114 us (0.65)
  other arithmetic: 56.7 us -> 5.38 us
  blocking collectives: 38.7 us -> 0 us
  starting transfers between devices: 4.26 us -> 27.1 us
  local copies, waits for them, and re-layouts: 43.5 us -> 54.9 us
  waiting for transfers between devices: 24.9 us -> 20 us
    unnamed x6 -> x5, other arithmetic: 47.7 us -> 0.27 us
    dynamic_update_slice x0 -> x8, local copies, waits for them, and re-layouts: none -> 39.2 us  [local(): whole = lax.dynamic_update_slice_in_dim(whole, other, source, axis=0)]
    all_to_all x1 -> x0, blocking collectives: 38.7 us -> none  [local(): lax.all_to_all(packed, 'row', split_axis=2, concat_axis=1, tiled=True)]
    unnamed x21 -> x20, local copies, waits for them, and re-layouts: 20 us -> 2.68 us
    ppermute x0 -> x7, starting transfers between devices: none -> 11.5 us  [local(): lax.ppermute(sent, 'row', [(i, (i + step) % size) for i in range(size)])]
    all_to_all x1, starting transfers between devices: 4.26 us -> 15.6 us  [local(): lax.all_to_all(derivative_lines, 'row', split_axis=1, concat_axis=2, tile...]
    all_to_all x1 -> x0, local copies, waits for them, and re-layouts: 10.6 us -> none  [local(): lax.all_to_all(packed, 'row', split_axis=2, concat_axis=1, tiled=True)]
    all_to_all x1, waiting for transfers between devices: 24.9 us -> 14.6 us  [local(): lax.all_to_all(derivative_lines, 'row', split_axis=1, concat_axis=2, tile...]
  transfers between devices with their start and end apart: 1 -> 8, of which waited for: 1 -> 3; matrix products, arithmetic and copies ran while one was open for 3% -> 35% of each run, Pallas kernels for 0% -> 0%
where the time goes in v1:
time: 114 us; the launch traced here: 113 us
  local copies, waits for them, and re-layouts  54.9 us (48%)
  starting transfers between devices  27.1 us (24%)
  waiting for transfers between devices  20 us (18%)
  other arithmetic  5.38 us (5%)
  matrix products  4.76 us (4%)
    dynamic_update_slice x8, local copies, waits for them, and re-layouts, local(): whole = lax.dynamic_update_slice_in_dim(whole, other, source, axis=0)  39.2 us
    all_to_all x1, starting transfers between devices, local(): lax.all_to_all(derivative_lines, 'row', split_axis=1, concat_axis=2, tile...  15.6 us
    all_to_all x1, waiting for transfers between devices, local(): lax.all_to_all(derivative_lines, 'row', split_axis=1, concat_axis=2, tile...  14.6 us
    ppermute x7, starting transfers between devices, local(): lax.ppermute(sent, 'row', [(i, (i + step) % size) for i in range(size)])  11.5 us
    ppermute x7, waiting for transfers between devices, local(): lax.ppermute(sent, 'row', [(i, (i + step) % size) for i in range(size)])  5.4 us
    dot_general x1, matrix products, compact_last(): jnp.einsum('...bj,jk->...bk', blocks, block_weights(count), precision=lax...  3.51 us
    neg x1, other arithmetic, local(): return -(derivative_x + derivative_y)  3.28 us
    unnamed x20, local copies, waits for them, and re-layouts  2.68 us
  transfers between devices with their start and end apart: 8, of which 3 were waited for; matrix products, arithmetic and copies ran while one was open for 35% of the time, Pallas kernels for 0%

profile of v1, /device:TPU:0, one launch (start us, length us, event | category | flops | bytes accessed | tf_op | source)
XLA Modules:
  0.0 112.6 jit_solution(368019086716041924)
XLA Ops:
  0.0 0.0 copy-start
  0.0 1.0 bitcast_dynamic-update-slice_fusion.9
  1.0 0.0 copy-start.1
  1.1 0.0 copy-start.2
  1.1 1.4 %multiply_reduce_fusion = (f32[32,2048]{1,0:T(8,128)S(1)}, f32[3,1,32,2048]{3,2,1,0:T(8,128)S(1)}) fusion(f32[3,1,32,2048]{3,2,1,0:T(8,128)} %param.6, f32[32,2048]{1,0:T(8,128)} %bitcast.128), kind=kLoop, calls=%fused_computation.7 | loop fusion | flops 524288 | bytes 2097152 | tf_op jit(solution)/shard_map/reduce_sum | solution.py:84
  2.5 0.0 copy-done
  2.5 0.0 copy-done.1
  2.5 0.0 copy-done.2
  2.5 0.1 bitcast_dynamic-update-slice_fusion.7
  2.7 2.1 %copy.18 = f32[1,32,5,2048]{3,2,1,0:T(8,128)} copy(f32[1,32,5,2048]{3,1,2,0:T(8,128)S(1)} %bitcast_dynamic-update-slice_fusion.5) | data formatting | bytes 2621440 | tf_op jit(solution)/shard_map/stack | solution.py:96
  4.8 1.8 %reshape_reshape.3 = f32[1,32,8,1280]{3,2,1,0:T(8,128)S(1)} reshape(f32[1,32,5,2048]{3,2,1,0:T(8,128)} %copy.18) | data formatting | bytes 2621440 | tf_op jit(solution)/shard_map/reshape;reshape | solution.py:10
  6.7 1.6 %dynamic-slice_bitcast_fusion = (f32[1,1,32,1280]{3,0,2,1:T(1,128)}, f32[1,1,32,1280]{3,0,2,1:T(1,128)}, f32[1,1,32,1280]{3,0,2,1:T(1,128)}, f32[1,1,32,1280]{3,...) fusion(f32[1,32,8,1280]{3,2,1,0:T(8,128)S(1)} %reshape_reshape.3, ...), kind=kLoop, calls=%fused_computation.33 | loop fusion | bytes 2293788 | tf_op jit(solution)/shard_map/jit(dynamic_index_in_dim)/dynamic_slice | solution.py:119
  8.3 3.0 %collective-permute-start.1 = (f32[1,1,32,1280]{3,0,2,1:T(1,128)S(1)}, f32[1,1,32,1280]{3,0,2,1:T(1,128)}, u32[]{:S(2)}, u32[]{:S(2)}) collective-permute-start(f32[1,1,32,1280]{3,0,2,1:T(1,128)S(1)} %get-tuple-element.18), channel_id=1, source_target_pairs={{0,8},{4,12},{8,16},{12,20},{16,24},{20,28},{24,0},{28,4},{1,9},{5... | collective-permute-start | bytes 491528 | tf_op jit(solution)/shard_map/ppermute | solution.py:120
  11.3 1.5 %collective-permute-start = (f32[1,1,32,1280]{3,0,2,1:T(1,128)S(1)}, f32[1,1,32,1280]{3,0,2,1:T(1,128)}, u32[]{:S(2)}, u32[]{:S(2)}) collective-permute-start(f32[1,1,32,1280]{3,0,2,1:T(1,128)S(1)} %get-tuple-element.19), channel_id=1, source_target_pairs={{0,4},{4,8},{8,12},{12,16},{16,20},{20,24},{24,28},{28,0},{1,5},{5... | collective-permute-start | bytes 491528 | tf_op jit(solution)/shard_map/ppermute | solution.py:120
  12.8 2.0 %collective-permute-start.4 = (f32[1,1,32,1280]{3,0,2,1:T(1,128)}, f32[1,1,32,1280]{3,0,2,1:T(1,128)}, u32[]{:S(2)}, u32[]{:S(2)}) collective-permute-start(f32[1,1,32,1280]{3,0,2,1:T(1,128)} %get-tuple-element.15), channel_id=1, source_target_pairs={{0,20},{4,24},{8,28},{12,0},{16,4},{20,8},{24,12},{28,16},{1,21},{... | collective-permute-start | bytes 491528 | tf_op jit(solution)/shard_map/ppermute | solution.py:120
  14.9 0.9 collective-permute-start.2
  15.8 2.6 %collective-permute-start.3 = (f32[1,1,32,1280]{3,0,2,1:T(1,128)}, f32[1,1,32,1280]{3,0,2,1:T(1,128)}, u32[]{:S(2)}, u32[]{:S(2)}) collective-permute-start(f32[1,1,32,1280]{3,0,2,1:T(1,128)} %get-tuple-element.16), channel_id=1, source_target_pairs={{0,16},{4,20},{8,24},{12,28},{16,0},{20,4},{24,8},{28,12},{1,17},{... | collective-permute-start | bytes 491528 | tf_op jit(solution)/shard_map/ppermute | solution.py:120
  18.4 0.0 collective-permute-done.1
  18.4 1.5 %collective-permute-start.5 = (f32[1,1,32,1280]{3,0,2,1:T(1,128)}, f32[1,1,32,1280]{3,0,2,1:T(1,128)}, u32[]{:S(2)}, u32[]{:S(2)}) collective-permute-start(f32[1,1,32,1280]{3,0,2,1:T(1,128)} %get-tuple-element.14), channel_id=1, source_target_pairs={{0,24},{4,28},{8,0},{12,4},{16,8},{20,12},{24,16},{28,20},{1,25},{... | collective-permute-start | bytes 491528 | tf_op jit(solution)/shard_map/ppermute | solution.py:120
  19.8 3.4 %collective-permute-done = f32[1,1,32,1280]{3,0,2,1:T(1,128)} collective-permute-done((f32[1,1,32,1280]{3,0,2,1:T(1,128)S(1)}, f32[1,1,32,1280]{3,0,2,1:T(1,128)}, u32[]{:S(2)}, u32[]{:S(2)}) %collective-permute-start) | collective-permute-done | bytes 163872 | tf_op jit(solution)/shard_map/ppermute | solution.py:120
  23.2 0.0 collective-permute-start.6
  23.2 5.5 %dynamic_update_slice.21 = f32[8,1,32,1280]{3,0,2,1:T(8,128)S(1)} dynamic-update-slice(f32[8,1,32,1280]{3,0,2,1:T(8,128)S(1)} %bitcast.119, f32[1,1,32,1280]{3,0,2,1:T(1,128)} %collective-permute-done, s32[]{:T(128)S(6)} %select_n.105, s32[]{:T(128)} %constant.107.clone.1, s32[]{:T(128)} %constant.107.clone.1, s32[]{:T(128)} %constant.107.clone.1) | dynamic-update-slice | bytes 327684 | tf_op jit(solution)/shard_map/dynamic_update_slice | solution.py:121
  28.7 5.6 %dynamic_update_slice.22 = f32[8,1,32,1280]{3,0,2,1:T(8,128)S(1)} dynamic-update-slice(f32[8,1,32,1280]{3,0,2,1:T(8,128)S(1)} %dynamic_update_slice.21, f32[1,1,32,1280]{3,0,2,1:T(1,128)} %collective-permute-done.1, s32[]{:T(128)S(6)} %select_n.109, s32[]{:T(128)} %constant.107.clone.1, s32[]{:T(128)} %constant.107.clone.1, s32[]{:T(128)} %constant.107.clone.1) | dynamic-update-slice | bytes 327684 | tf_op jit(solution)/shard_map/dynamic_update_slice | solution.py:121
  34.3 2.0 %collective-permute-done.2 = f32[1,1,32,1280]{3,0,2,1:T(1,128)} collective-permute-done((f32[1,1,32,1280]{3,0,2,1:T(1,128)}, f32[1,1,32,1280]{3,0,2,1:T(1,128)}, u32[]{:S(2)}, u32[]{:S(2)}) %collective-permute-start.2) | collective-permute-done | bytes 163872 | tf_op jit(solution)/shard_map/ppermute | solution.py:120
  36.3 5.5 %dynamic_update_slice.23 = f32[8,1,32,1280]{3,0,2,1:T(8,128)S(1)} dynamic-update-slice(f32[8,1,32,1280]{3,0,2,1:T(8,128)S(1)} %dynamic_update_slice.22, f32[1,1,32,1280]{3,0,2,1:T(1,128)} %collective-permute-done.2, s32[]{:T(128)S(6)} %select_n.113, s32[]{:T(128)} %constant.107.clone.1, s32[]{:T(128)} %constant.107.clone.1, s32[]{:T(128)} %constant.107.clone.1) | dynamic-update-slice | bytes 327684 | tf_op jit(solution)/shard_map/dynamic_update_slice | solution.py:121
  41.8 0.0 collective-permute-done.3
  41.8 5.6 %dynamic_update_slice.24 = f32[8,1,32,1280]{3,0,2,1:T(8,128)S(1)} dynamic-update-slice(f32[8,1,32,1280]{3,0,2,1:T(8,128)S(1)} %dynamic_update_slice.23, f32[1,1,32,1280]{3,0,2,1:T(1,128)} %collective-permute-done.3, s32[]{:T(128)S(6)} %select_n.117, s32[]{:T(128)} %constant.107.clone.1, s32[]{:T(128)} %constant.107.clone.1, s32[]{:T(128)} %constant.107.clone.1) | dynamic-update-slice | bytes 327684 | tf_op jit(solution)/shard_map/dynamic_update_slice | solution.py:121
  47.4 0.0 collective-permute-done.4
  47.4 5.6 %dynamic_update_slice.25 = f32[8,1,32,1280]{3,0,2,1:T(8,128)S(1)} dynamic-update-slice(f32[8,1,32,1280]{3,0,2,1:T(8,128)S(1)} %dynamic_update_slice.24, f32[1,1,32,1280]{3,0,2,1:T(1,128)} %collective-permute-done.4, s32[]{:T(128)S(6)} %select_n.121, s32[]{:T(128)} %constant.107.clone.1, s32[]{:T(128)} %constant.107.clone.1, s32[]{:T(128)} %constant.107.clone.1) | dynamic-update-slice | bytes 327684 | tf_op jit(solution)/shard_map/dynamic_update_slice | solution.py:121
  53.0 0.0 collective-permute-done.5
  53.0 5.6 %dynamic_update_slice.26 = f32[8,1,32,1280]{3,0,2,1:T(8,128)S(1)} dynamic-update-slice(f32[8,1,32,1280]{3,0,2,1:T(8,128)S(1)} %dynamic_update_slice.25, f32[1,1,32,1280]{3,0,2,1:T(1,128)} %collective-permute-done.5, s32[]{:T(128)S(6)} %select_n.125, s32[]{:T(128)} %constant.107.clone.1, s32[]{:T(128)} %constant.107.clone.1, s32[]{:T(128)} %constant.107.clone.1) | dynamic-update-slice | bytes 327684 | tf_op jit(solution)/shard_map/dynamic_update_slice | solution.py:121
  58.5 0.0 collective-permute-done.6
  58.5 5.6 %dynamic_update_slice.27 = f32[8,1,32,1280]{3,0,2,1:T(8,128)S(1)} dynamic-update-slice(f32[8,1,32,1280]{3,0,2,1:T(8,128)S(1)} %dynamic_update_slice.26, f32[1,1,32,1280]{3,0,2,1:T(1,128)} %collective-permute-done.6, s32[]{:T(128)S(6)} %select_n.129, s32[]{:T(128)} %constant.107.clone.1, s32[]{:T(128)} %constant.107.clone.1, s32[]{:T(128)} %constant.107.clone.1) | dynamic-update-slice | bytes 327684 | tf_op jit(solution)/shard_map/dynamic_update_slice | solution.py:121
  64.1 0.0 copy-start.3
  64.1 0.4 copy.19
  64.6 0.5 copy-done.3
  65.1 1.3 %convolution_bitcast_fusion = f32[1,256,1280]{2,1,0:T(8,128)S(1)} fusion(f32[256,256]{1,0:T(8,128)S(1)} %copy-done.3, f32[256,1280]{1,0:T(8,128)S(1)} %bitcast.121), kind=kOutput, calls=%fused_computation | convolution fusion | flops 1006632960 | bytes 2883584 | tf_op jit(solution)/shard_map/...jc,ji->...ic/dot_general | solution.py:68
  66.3 2.4 %copy.20 = f32[1,256,1280]{2,0,1:T(1,128)} copy(f32[1,256,1280]{2,1,0:T(8,128)S(1)} %convolution_bitcast_fusion) | data formatting | bytes 2621440 | tf_op jit(solution)/shard_map/...jc,ji->...ic/transpose | solution.py:68
  68.8 15.6 %all-to-all-start = ((f32[1,256,1280]{2,0,1:T(1,128)}), f32[1,256,1280]{2,0,1:T(1,128)S(1)}, u32[]{:S(2)}, u32[]{:S(2)}) async-start(f32[1,256,1280]{2,0,1:T(1,128)} %copy.20), calls=%async_computation | async-start | bytes 2621440 | tf_op jit(solution)/shard_map/all_to_all | solution.py:124
  84.4 0.1 multiply_bitcast_fusion
  84.6 0.1 fusion.7
  84.8 0.0 copy-start.4
  85.0 0.8 copy-done.4
  85.8 3.5 %convolution_bitcast_fusion.1 = f32[5,1,32,16,384]{4,3,2,0,1:T(8,128)S(1)} fusion(f32[5,32,16,128]{3,2,1,0:T(8,128)S(1)} %bitcast_dynamic-update-slice_fusion, f32[128,384,1,1]{1,0,3,2:T(8,128)S(1)} %copy-done.4), kind=kOutput, calls=%fused_computation.1 | convolution fusion | flops 1509949440 | bytes 5439488 | tf_op jit(solution)/shard_map/...bj,jk->...bk/dot_general | solution.py:53
  89.3 0.1 fusion.10
  89.4 0.2 fusion.9
  89.6 0.4 fusion
  90.0 1.3 %reshape.141 = f32[5,1,32,2048]{3,2,1,0:T(8,128)} reshape(f32[5,1,32,16,128]{4,3,2,0,1:T(8,128)S(1)} %fusion) | data formatting | bytes 2621440 | tf_op jit(solution)/shard_map/reshape | solution.py:61
  91.3 14.6 %all-to-all-done = f32[1,256,1280]{2,0,1:T(1,128)S(1)} async-done(((f32[1,256,1280]{2,0,1:T(1,128)}), f32[1,256,1280]{2,0,1:T(1,128)S(1)}, u32[]{:S(2)}, u32[]{:S(2)}) %all-to-all-start) | async-done | bytes 1310752 | tf_op jit(solution)/shard_map/all_to_all | solution.py:124
  105.9 1.9 %copy.31 = f32[1,8,32,1280]{3,1,2,0:T(8,128)} copy(f32[1,8,32,1280]{3,0,2,1:T(1,128)S(1)} %bitcast.120) | data formatting | bytes 2621440 | tf_op jit(solution)/shard_map/all_to_all | solution.py:124
  107.8 1.5 %reshape.143 = f32[1,32,5,2048]{3,2,1,0:T(8,128)S(1)} reshape(f32[1,32,8,1280]{3,2,1,0:T(8,128)} %bitcast.122) | data formatting | bytes 2621440 | tf_op jit(solution)/shard_map/reshape | solution.py:125
  109.3 3.3 %fusion.1 = f32[5,1,32,2048]{3,2,1,0:T(8,128)} fusion(f32[5,1,32,2048]{3,2,1,0:T(8,128)} %reshape.141, f32[1,32,5,2048]{3,2,1,0:T(8,128)S(1)} %reshape.143), kind=kLoop, calls=%fused_computation.5 | loop fusion | flops 655360 | bytes 3932160 | tf_op jit(solution)/shard_map/neg | solution.py:126
  (13 shorter events, 0.4 us)
Async XLA Ops:
  0.0 2.5 %copy-start = (f32[3,1,32,2048]{3,2,1,0:T(8,128)S(1)}, f32[3,1,32,2048]{3,2,1,0:T(8,128)}, u32[]{:S(2)}) copy-start(f32[3,1,32,2048]{3,2,1,0:T(8,128)} %param.6) | copy-start | bytes 2359300
  1.0 1.5 %copy-start.1 = (f32[1,32,2048]{2,1,0:T(8,128)S(1)}, f32[1,32,2048]{2,1,0:T(8,128)}, u32[]{:S(2)}) copy-start(f32[1,32,2048]{2,1,0:T(8,128)} %param.7) | copy-start | bytes 786436
  1.1 1.5 %copy-start.2 = (f32[1,32,2048]{2,1,0:T(8,128)S(1)}, f32[1,32,2048]{2,1,0:T(8,128)}, u32[]{:S(2)}) copy-start(f32[1,32,2048]{2,1,0:T(8,128)} %param.5) | copy-start | bytes 786436
  8.3 10.1 %collective-permute-start.1 = (f32[1,1,32,1280]{3,0,2,1:T(1,128)S(1)}, f32[1,1,32,1280]{3,0,2,1:T(1,128)}, u32[]{:S(2)}, u32[]{:S(2)}) collective-permute-start(f32[1,1,32,1280]{3,0,2,1:T(1,128)S(1)} %get-tuple-element.18), channel_id=1, source_target_pairs={{0,8},{4,12},{8,16},{12,20},{16,24},{20,28},{24,0},{28,4},{1,9},{5... | collective-permute-start | bytes 491528 | tf_op jit(solution)/shard_map/ppermute | solution.py:120
  11.3 11.9 %collective-permute-start = (f32[1,1,32,1280]{3,0,2,1:T(1,128)S(1)}, f32[1,1,32,1280]{3,0,2,1:T(1,128)}, u32[]{:S(2)}, u32[]{:S(2)}) collective-permute-start(f32[1,1,32,1280]{3,0,2,1:T(1,128)S(1)} %get-tuple-element.19), channel_id=1, source_target_pairs={{0,4},{4,8},{8,12},{12,16},{16,20},{20,24},{24,28},{28,0},{1,5},{5... | collective-permute-start | bytes 491528 | tf_op jit(solution)/shard_map/ppermute | solution.py:120
  12.8 34.5 %collective-permute-start.4 = (f32[1,1,32,1280]{3,0,2,1:T(1,128)}, f32[1,1,32,1280]{3,0,2,1:T(1,128)}, u32[]{:S(2)}, u32[]{:S(2)}) collective-permute-start(f32[1,1,32,1280]{3,0,2,1:T(1,128)} %get-tuple-element.15), channel_id=1, source_target_pairs={{0,20},{4,24},{8,28},{12,0},{16,4},{20,8},{24,12},{28,16},{1,21},{... | collective-permute-start | bytes 491528 | tf_op jit(solution)/shard_map/ppermute | solution.py:120
  14.9 21.4 %collective-permute-start.2 = (f32[1,1,32,1280]{3,0,2,1:T(1,128)}, f32[1,1,32,1280]{3,0,2,1:T(1,128)}, u32[]{:S(2)}, u32[]{:S(2)}) collective-permute-start(f32[1,1,32,1280]{3,0,2,1:T(1,128)} %get-tuple-element.17), channel_id=1, source_target_pairs={{0,12},{4,16},{8,20},{12,24},{16,28},{20,0},{24,4},{28,8},{1,13},{... | collective-permute-start | bytes 491528 | tf_op jit(solution)/shard_map/ppermute | solution.py:120
  15.8 26.0 %collective-permute-start.3 = (f32[1,1,32,1280]{3,0,2,1:T(1,128)}, f32[1,1,32,1280]{3,0,2,1:T(1,128)}, u32[]{:S(2)}, u32[]{:S(2)}) collective-permute-start(f32[1,1,32,1280]{3,0,2,1:T(1,128)} %get-tuple-element.16), channel_id=1, source_target_pairs={{0,16},{4,20},{8,24},{12,28},{16,0},{20,4},{24,8},{28,12},{1,17},{... | collective-permute-start | bytes 491528 | tf_op jit(solution)/shard_map/ppermute | solution.py:120
  18.4 34.6 %collective-permute-start.5 = (f32[1,1,32,1280]{3,0,2,1:T(1,128)}, f32[1,1,32,1280]{3,0,2,1:T(1,128)}, u32[]{:S(2)}, u32[]{:S(2)}) collective-permute-start(f32[1,1,32,1280]{3,0,2,1:T(1,128)} %get-tuple-element.14), channel_id=1, source_target_pairs={{0,24},{4,28},{8,0},{12,4},{16,8},{20,12},{24,16},{28,20},{1,25},{... | collective-permute-start | bytes 491528 | tf_op jit(solution)/shard_map/ppermute | solution.py:120
  23.2 35.3 %collective-permute-start.6 = (f32[1,1,32,1280]{3,0,2,1:T(1,128)}, f32[1,1,32,1280]{3,0,2,1:T(1,128)}, u32[]{:S(2)}, u32[]{:S(2)}) collective-permute-start(f32[1,1,32,1280]{3,0,2,1:T(1,128)} %get-tuple-element.13), channel_id=1, source_target_pairs={{0,28},{4,0},{8,4},{12,8},{16,12},{20,16},{24,20},{28,24},{1,29},{... | collective-permute-start | bytes 491528 | tf_op jit(solution)/shard_map/ppermute | solution.py:120
  64.1 1.0 copy-start.3
  68.8 37.1 %all-to-all-start = ((f32[1,256,1280]{2,0,1:T(1,128)}), f32[1,256,1280]{2,0,1:T(1,128)S(1)}, u32[]{:S(2)}, u32[]{:S(2)}) async-start(f32[1,256,1280]{2,0,1:T(1,128)} %copy.20), calls=%async_computation | async-start | bytes 2621440 | tf_op jit(solution)/shard_map/all_to_all | solution.py:124
  84.8 0.9 copy-start.4
